TPU v7x, 128 devices: a whole 4x4x4 slice. The times are simulated.
128 devices in a mesh: row: 8 (over y, core), col: 16 (over x, z).
Axes of the slice: x: 4, y: 4, z: 4, core: 2. Of those that a mesh axis runs over, the one named last changes fastest.
Arguments:
- tokens: bfloat16 [10240, 3200], P('col', 'row'), may hold values from -24 to 24
- w_qkv: bfloat16 [3200, 9600], P('row', 'col'), may hold values from -4 to 4
- q_gain: float32 [3200], replicated, may hold values from 0.5 to 1.5
- k_gain: float32 [3200], replicated, may hold values from 0.5 to 1.5
- segment_ids: int32 [8, 1280], P('row'), may hold values from 0 to 3, never falling along the last dimension, each value on 1 to 640 neighbouring positions
Outputs:
- attended: bfloat16 [10240, 3200], P(('row', 'col'))
Inputs may be any that keep to these rules, and one draw needn't show every extreme that they name: `segment_ids`: in each pack the ids never fall; each of the 4 images holds 1 to 640 tokens, one exactly 640.
All inputs are finite; a program needn't handle non-finite values.
Results may differ from a plain program's by a relative error of at most 0.033.
Values may be sent and summed in bfloat16 or wider, within the bound.
No kernel may reach another device: no remote copies, remote signals or barrier semaphores. Data moves between devices by JAX's collectives and lax.ppermute only.
A program may use at most 192 MiB of HBM per device.

v0:
```python
import jax
import jax.numpy as jnp
from jax import lax
from jax.sharding import PartitionSpec as P

ATTENTION_HEADS = 25
HEAD_WIDTH = 128
TOK_DEV = 80


def rms_norm(block, gain):
    values = block.astype(jnp.float32)
    mean_sq = jnp.mean(values * values, axis=-1, keepdims=True)
    return (values * lax.rsqrt(mean_sq + 1e-06) * gain).astype(jnp.bfloat16)


def attend(carry, queries, query_ids, keys, values, key_ids):
    best, total, accum = carry
    count_q = queries.shape[0]
    count_k = keys.shape[0]
    q3 = queries.reshape(count_q, ATTENTION_HEADS, HEAD_WIDTH)
    k3 = keys.reshape(count_k, ATTENTION_HEADS, HEAD_WIDTH)
    value_three = values.reshape(count_k, ATTENTION_HEADS, HEAD_WIDTH)
    scores = jnp.einsum(
        "qhd,khd->hqk", q3, k3, preferred_element_type=jnp.float32
    ) * HEAD_WIDTH ** (-0.5)
    mask = (query_ids[:, None] == key_ids[None, :])[None]
    masked = jnp.where(mask, scores, -1e30)
    new_best = jnp.maximum(best, jnp.max(masked, axis=-1))
    expo = jnp.where(mask, jnp.exp(masked - new_best[..., None]), 0.0)
    ratio = jnp.exp(best - new_best)
    total = total * ratio + jnp.sum(expo, axis=-1)
    weights = expo.astype(jnp.bfloat16)
    update = jnp.einsum("hqk,khd->hqd", weights, value_three, preferred_element_type=jnp.float32)
    return (new_best, total, accum * ratio[..., None] + update)


def local(tokens, w_qkv, q_gain, k_gain, segment_ids):
    width = q_gain.shape[0]
    tok_count = TOK_DEV
    position = lax.axis_index("col")
    partial_sums = jnp.dot(
        lax.all_gather(tokens, "col", axis=0, tiled=True), w_qkv, preferred_element_type=jnp.float32
    )
    summed = lax.psum_scatter(
        partial_sums.astype(jnp.bfloat16), "row", scatter_dimension=0, tiled=True
    )
    pack_ids = segment_ids[0]
    query_ids = lax.dynamic_slice_in_dim(pack_ids, position * tok_count, tok_count, 0)
    start_carry = (
        jnp.full((ATTENTION_HEADS, tok_count), -1e30, jnp.float32),
        jnp.zeros((ATTENTION_HEADS, tok_count), jnp.float32),
        jnp.zeros((ATTENTION_HEADS, tok_count, HEAD_WIDTH), jnp.float32),
    )
    whole = lax.all_gather(summed, "col", axis=1, tiled=True)
    own_rows = lax.dynamic_slice_in_dim(whole, position * tok_count, tok_count, 0)
    normed_q = rms_norm(own_rows[:, :width], q_gain)
    normed_k = rms_norm(whole[:, width : 2 * width], k_gain)
    all_values = whole[:, 2 * width :]
    block_rows = whole.shape[0] // 4
    carry = start_carry
    for block in range(4):
        lower = block * block_rows
        keys = normed_k[lower : lower + block_rows]
        key_ids = lax.dynamic_slice_in_dim(pack_ids, lower, keys.shape[0], 0)
        carry = attend(
            carry, normed_q, query_ids, keys, all_values[lower : lower + block_rows], key_ids
        )
    best, total, accum = carry
    result = accum / total[..., None]
    return jnp.transpose(result, (1, 0, 2)).reshape(tok_count, width).astype(jnp.bfloat16)


def solution(mesh):
    return jax.shard_map(
        local,
        mesh=mesh,
        in_specs=(P("col", "row"), P("row", "col"), P(), P(), P("row", None)),
        out_specs=P(("row", "col"), None),
        check_vma=False,
    )
```

profile of v0, /device:TPU:1, one launch (start us, length us, event | category | flops | bytes accessed | tf_op | source)
XLA Modules:
  0.0 368.6 jit_solution(6712530993973618767)
XLA Ops:
  6.5 0.7 all-gather.3.cloned.1.call-update
  7.3 0.0 reduce-scatter.2.cloned.1.call-start
  7.3 75.2 %all-gather.3.cloned.1.call-done = bf16[10240,400]{0,1:T(8,128)(2,1)} async-done(((bf16[640,400]{0,1:T(8,128)(2,1)}), bf16[10240,400]{0,1:T(8,128)(2,1)}) %all-gather.3.cloned.1.call-update) | async-done | bytes 8192016 | tf_op jit(solution)/shard_map/all_gather | solution.py:43
  82.6 11.5 %convolution_convert_fusion = bf16[10240,600]{0,1:T(8,128)(2,1)} fusion(bf16[10240,400]{0,1:T(8,128)(2,1)} %all-gather.3.cloned.1.call-done, bf16[400,600]{1,0:T(8,128)(2,1)S(1)} %copy-done), kind=kOutput, calls=%fused_computation.5 | convolution fusion | flops 4921344000 | bytes 20960000 | tf_op jit(solution)/shard_map/dot_general | solution.py:42
  94.1 0.0 reduce-scatter.2.cloned.1.call-update
  94.1 0.0 all-gather.5.cloned.1.call-start
  94.1 70.5 %reduce-scatter.2.cloned.1.call-done = bf16[1280,600]{0,1:T(8,128)(2,1)} async-done(((bf16[10240,600]{0,1:T(8,128)(2,1)}), bf16[1280,600]{0,1:T(8,128)(2,1)}) %reduce-scatter.2.cloned.1.call-update) | async-done | bytes 1536016 | tf_op jit(solution)/shard_map/reduce_scatter | solution.py:45
  164.6 0.0 all-gather.5.cloned.1.call-update
  164.6 0.1 dynamic-slice_bitcast_fusion
  164.7 0.1 slice_reduce_fusion
  164.8 0.1 broadcast_compare_fusion.1
  164.9 153.1 %all-gather.5.cloned.1.call-done = bf16[1280,9600]{0,1:T(8,128)(2,1)} async-done(((bf16[1280,600]{0,1:T(8,128)(2,1)}), bf16[1280,9600]{0,1:T(8,128)(2,1)}) %all-gather.5.cloned.1.call-update) | async-done | bytes 24576016 | tf_op jit(solution)/shard_map/all_gather | solution.py:55
  318.0 1.9 fusion.15
  320.0 0.0 copy-start.3
  320.0 5.0 %fusion = f32[1280]{0:T(1024)S(1)} fusion(bf16[1280,9600]{0,1:T(8,128)(2,1)} %all-gather.5.cloned.1.call-done), kind=kLoop, calls=%fused_computation.2 | loop fusion | flops 12286720 | bytes 8197120 | tf_op jit(solution)/shard_map/reduce_sum | solution.py:13
  325.0 5.4 %fusion.2 = bf16[1280,3200]{0,1:T(8,128)(2,1)S(1)} fusion(f32[3200]{0:T(1024)S(1)} %copy-done.3, f32[1280]{0:T(1024)S(1)} %add_rsqrt_fusion, bf16[1280,9600]{0,1:T(8,128)(2,1)} %all-gather.5.cloned.1.call-done), kind=kLoop, calls=%fused_computation.4 | loop fusion | flops 16384000 | bytes 16401920 | tf_op jit(solution)/shard_map/convert_element_type | solution.py:14
  330.4 0.0 copy-start.2
  330.4 3.3 fusion.108
  333.7 2.1 fusion.17
  335.8 0.9 fusion.6
  336.8 0.9 fusion.5
  337.7 0.9 fusion.4
  338.6 0.9 fusion.3
  339.5 2.5 fusion.11
  342.0 2.5 fusion.7
  344.6 5.7 %fusion.107 = (bf16[320,3200]{0,1:T(8,128)(2,1)S(1)}, bf16[320,3200]{0,1:T(8,128)(2,1)S(1)}, bf16[320,3200]{0,1:T(8,128)(2,1)S(1)}, bf16[320,3200]{0,1:T(8,128)(2,1)S(1)}) fusion(bf16[1280,9600]{0,1:T(8,128)(2,1)} %all-gather.5.cloned.1.call-done), kind=kLoop, calls=%fused_computation.112 | loop fusion | bytes 16384000 | tf_op jit(solution)/shard_map/slice | solution.py:67
  350.3 2.7 fusion.76
  352.9 2.9 fusion.70
  355.8 2.7 fusion.64
  358.5 0.0 copy-start.1
  358.5 2.7 fusion.81
  361.2 0.9 copy.45
  (12 shorter events, 0.1 us)
Async XLA Ops:
  6.5 76.0 %copy-start = (bf16[400,600]{1,0:T(8,128)(2,1)S(1)}, bf16[400,600]{1,0:T(8,128)(2,1)}, u32[]{:S(2)}) copy-start(bf16[400,600]{1,0:T(8,128)(2,1)} %param.6) | copy-start | bytes 1440004
  6.5 76.0 %all-gather.3.cloned.1.call-start = ((), (), s32[]{:S(2)}) async-start(), calls=%async_computation.1 | async-start | bytes 8704000 | tf_op jit(solution)/shard_map/all_gather | solution.py:43
  7.3 157.3 %reduce-scatter.2.cloned.1.call-start = ((), (), s32[]{:S(2)}) async-start(), calls=%async_computation.2 | async-start | bytes 13824000 | tf_op jit(solution)/shard_map/reduce_scatter | solution.py:45
  94.1 70.6 %copy-start.4 = (s32[1,1280]{1,0:T(1,128)S(1)}, s32[1,1280]{1,0:T(1,128)}, u32[]{:S(2)}) copy-start(s32[1,1280]{1,0:T(1,128)} %param.9) | copy-start | bytes 15364
  94.1 224.0 %all-gather.5.cloned.1.call-start = ((), (), s32[]{:S(2)}) async-start(), calls=%async_computation.3 | async-start | bytes 26112000 | tf_op jit(solution)/shard_map/all_gather | solution.py:55
  320.0 5.0 %copy-start.3 = (f32[3200]{0:T(1024)S(1)}, f32[3200]{0:T(1024)}, u32[]{:S(2)}) copy-start(f32[3200]{0:T(1024)} %param.8) | copy-start | bytes 38404
  330.4 3.3 copy-start.2
  358.5 3.6 copy-start.1
Sparse Core Ops, SparseCore 0:
  9.5 72.9 all-gather.2
  94.2 70.3 reduce-scatter.1
  166.8 151.1 all-gather.4
where the time goes:
time: 369 us
  waiting for transfers between devices  300 us (81%)
  matrix products  26.1 us (7%)
  other arithmetic  19.7 us (5%)
  between operations  13.3 us (4%)
  local copies, waits for them, and re-layouts  9.99 us (3%)
    all_gather x1, waiting for transfers between devices, local(): whole = lax.all_gather(summed, 'col', axis=1, tiled=True)  153 us
    all_gather x1, waiting for transfers between devices, local(): lax.all_gather(tokens, 'col', axis=0, tiled=True)  75.2 us
    reduce_scatter x1, waiting for transfers between devices, local(): lax.psum_scatter(partial_sums.astype(jnp.bfloat16), 'row', scatter_dimens...  70.5 us
    dot_general x1, matrix products, local(): jnp.dot(lax.all_gather(tokens, 'col', axis=0, tiled=True), w_qkv, preferr...  11.5 us
    dot_general x4, matrix products, attend(): jnp.einsum('hqk,khd->hqd', weights, value_three, preferred_element_type=j...  10.9 us
    convert_element_type x2, other arithmetic, rms_norm(): return (values * lax.rsqrt(mean_sq + 1e-06) * gain).astype(jnp.bfloat16)  7.52 us
  transfers between devices with their start and end apart: 3, of which 3 were waited for; matrix products, arithmetic and copies ran while one was open for 0% of the time, Pallas kernels for 0%

commit v1 on v0

--- a/solution.py
+++ b/solution.py
@@ -1,3 +1,4 @@
+import functools
 import jax
 import jax.numpy as jnp
 from jax import lax
@@ -6,6 +7,15 @@
 ATTENTION_HEADS = 25
 HEAD_WIDTH = 128
 TOK_DEV = 80
+
+
+def vector_draw(raw, lane_axis):
+    tile_out = jnp.stack([raw for _ in range(jax.lax.axis_size(lane_axis))], axis=0)
+    everything = jax.lax.all_to_all(tile_out, lane_axis, split_axis=0, concat_axis=0)
+    return jnp.concatenate(everything, 0)
+
+
+update_area_on_mesh = functools.partial(vector_draw, lane_axis="col")
 
 
 def rms_norm(block, gain):
@@ -39,9 +49,7 @@
     width = q_gain.shape[0]
     tok_count = TOK_DEV
     position = lax.axis_index("col")
-    partial_sums = jnp.dot(
-        lax.all_gather(tokens, "col", axis=0, tiled=True), w_qkv, preferred_element_type=jnp.float32
-    )
+    partial_sums = jnp.dot(update_area_on_mesh(tokens), w_qkv, preferred_element_type=jnp.float32)
     summed = lax.psum_scatter(
         partial_sums.astype(jnp.bfloat16), "row", scatter_dimension=0, tiled=True
     )

time: 369 us -> 404 us (1.095)
  blocking collectives: 0 us -> 101 us
  waiting for transfers between devices: 300 us -> 224 us
  local copies, waits for them, and re-layouts: 9.99 us -> 19.5 us
    all_to_all x0 -> x1, blocking collectives: none -> 101 us  [vector_draw(): jax.lax.all_to_all(tile_out, lane_axis, split_axis=0, concat_axis=0)]
    all_gather x1 -> x0, waiting for transfers between devices: 75.2 us -> none  [local(): lax.all_gather(tokens, 'col', axis=0, tiled=True)]
    reshape x0 -> x1, local copies, waits for them, and re-layouts: none -> 7.78 us  [vector_draw(): return jnp.concatenate(everything, 0)]
  transfers between devices with their start and end apart: 3 -> 2, of which waited for: 3 -> 2; matrix products, arithmetic and copies ran while one was open for 0% -> 0% of each run, Pallas kernels for 0% -> 0%
where the time goes in v1:
time: 404 us
  waiting for transfers between devices  224 us (55%)
  blocking collectives  101 us (25%)
  matrix products  26.1 us (6%)
  other arithmetic  19.7 us (5%)
  local copies, waits for them, and re-layouts  19.5 us (5%)
  between operations  13.6 us (3%)
    all_gather x1, waiting for transfers between devices, local(): whole = lax.all_gather(summed, 'col', axis=1, tiled=True)  153 us
    all_to_all x1, blocking collectives, vector_draw(): jax.lax.all_to_all(tile_out, lane_axis, split_axis=0, concat_axis=0)  101 us
    reduce_scatter x1, waiting for transfers between devices, local(): lax.psum_scatter(partial_sums.astype(jnp.bfloat16), 'row', scatter_dimens...  70.9 us
    dot_general x1, matrix products, local(): jnp.dot(update_area_on_mesh(tokens), w_qkv, preferred_element_type=jnp.fl...  11.5 us
    dot_general x4, matrix products, attend(): jnp.einsum('hqk,khd->hqd', weights, value_three, preferred_element_type=j...  10.9 us
  transfers between devices with their start and end apart: 2, of which 2 were waited for; matrix products, arithmetic and copies ran while one was open for 0% of the time, Pallas kernels for 0%

profile of v1, /device:TPU:1, one launch (start us, length us, event | category | flops | bytes accessed | tf_op | source)
XLA Modules:
  0.0 404.1 jit_solution(3491407167615124131)
XLA Ops:
  6.5 1.7 stack.2
  8.3 101.3 %all_to_all.5 = bf16[16,640,400]{1,2,0:T(8,128)(2,1)} all-to-all(bf16[16,640,400]{1,2,0:T(8,128)(2,1)S(1)} %stack.2), channel_id=1, replica_groups=mesh['row'=8,'col'=16] {'col'}, dimensions={0} | all-to-all | bytes 16384000 | tf_op jit(solution)/shard_map/all_to_all | solution.py:14
  109.6 7.8 %copy.72 = bf16[16,50,8,640]{3,2,0,1:T(8,128)(2,1)} copy(bf16[16,50,8,640]{3,2,1,0:T(8,128)(2,1)} %bitcast.123) | data formatting | bytes 16384000 | tf_op jit(solution)/shard_map/reshape | solution.py:15
  117.3 11.5 %convolution_convert_fusion = bf16[10240,600]{0,1:T(8,128)(2,1)} fusion(bf16[10240,400]{0,1:T(8,128)(2,1)} %bitcast.132, bf16[400,600]{1,0:T(8,128)(2,1)S(1)} %copy-done), kind=kOutput, calls=%fused_computation.5 | convolution fusion | flops 4921344000 | bytes 20960000 | tf_op jit(solution)/shard_map/dot_general | solution.py:52
  128.8 0.0 reduce-scatter.2.cloned.1.call-update
  128.9 0.0 all-gather.2.cloned.1.call-start
  128.9 70.9 %reduce-scatter.2.cloned.1.call-done = bf16[1280,600]{0,1:T(8,128)(2,1)} async-done(((bf16[10240,600]{0,1:T(8,128)(2,1)}), bf16[1280,600]{0,1:T(8,128)(2,1)}) %reduce-scatter.2.cloned.1.call-update) | async-done | bytes 1536016 | tf_op jit(solution)/shard_map/reduce_scatter | solution.py:53
  199.8 0.0 all-gather.2.cloned.1.call-update
  199.9 0.1 dynamic-slice_bitcast_fusion
  199.9 0.1 slice_reduce_fusion
  200.0 0.1 broadcast_compare_fusion.1
  200.2 153.1 %all-gather.2.cloned.1.call-done = bf16[1280,9600]{0,1:T(8,128)(2,1)} async-done(((bf16[1280,600]{0,1:T(8,128)(2,1)}), bf16[1280,9600]{0,1:T(8,128)(2,1)}) %all-gather.2.cloned.1.call-update) | async-done | bytes 24576016 | tf_op jit(solution)/shard_map/all_gather | solution.py:63
  353.3 1.9 fusion.15
  355.2 0.0 copy-start.3
  355.2 5.0 %fusion = f32[1280]{0:T(1024)S(1)} fusion(bf16[1280,9600]{0,1:T(8,128)(2,1)} %all-gather.2.cloned.1.call-done), kind=kLoop, calls=%fused_computation.2 | loop fusion | flops 12286720 | bytes 8197120 | tf_op jit(solution)/shard_map/reduce_sum | solution.py:23
  360.2 5.4 %fusion.2 = bf16[1280,3200]{0,1:T(8,128)(2,1)S(1)} fusion(f32[3200]{0:T(1024)S(1)} %copy-done.3, f32[1280]{0:T(1024)S(1)} %add_rsqrt_fusion, bf16[1280,9600]{0,1:T(8,128)(2,1)} %all-gather.2.cloned.1.call-done), kind=kLoop, calls=%fused_computation.4 | loop fusion | flops 16384000 | bytes 16401920 | tf_op jit(solution)/shard_map/convert_element_type | solution.py:24
  365.6 0.0 copy-start.2
  365.6 3.3 fusion.108
  368.9 2.1 fusion.17
  371.1 0.9 fusion.6
  372.0 0.9 fusion.5
  372.9 0.9 fusion.4
  373.8 0.9 fusion.3
  374.7 2.5 fusion.11
  377.3 2.5 fusion.7
  379.8 5.7 %fusion.107 = (bf16[320,3200]{0,1:T(8,128)(2,1)S(1)}, bf16[320,3200]{0,1:T(8,128)(2,1)S(1)}, bf16[320,3200]{0,1:T(8,128)(2,1)S(1)}, bf16[320,3200]{0,1:T(8,128)(2,1)S(1)}) fusion(bf16[1280,9600]{0,1:T(8,128)(2,1)} %all-gather.2.cloned.1.call-done), kind=kLoop, calls=%fused_computation.112 | loop fusion | bytes 16384000 | tf_op jit(solution)/shard_map/slice | solution.py:75
  385.5 2.7 fusion.76
  388.2 2.9 fusion.70
  391.0 2.7 fusion.64
  393.7 0.0 copy-start.1
  393.7 2.7 fusion.81
  396.4 0.9 copy.75
  (12 shorter events, 0.1 us)
Async XLA Ops:
  6.5 110.8 %copy-start = (bf16[400,600]{1,0:T(8,128)(2,1)S(1)}, bf16[400,600]{1,0:T(8,128)(2,1)}, u32[]{:S(2)}) copy-start(bf16[400,600]{1,0:T(8,128)(2,1)} %param.6) | copy-start | bytes 1440004
  6.5 193.3 %reduce-scatter.2.cloned.1.call-start = ((), (), s32[]{:S(2)}) async-start(), calls=%async_computation.2 | async-start | bytes 13824000 | tf_op jit(solution)/shard_map/reduce_scatter | solution.py:53
  128.8 71.0 %copy-start.4 = (s32[1,1280]{1,0:T(1,128)S(1)}, s32[1,1280]{1,0:T(1,128)}, u32[]{:S(2)}) copy-start(s32[1,1280]{1,0:T(1,128)} %param.9) | copy-start | bytes 15364
  128.9 224.4 %all-gather.2.cloned.1.call-start = ((), (), s32[]{:S(2)}) async-start(), calls=%async_computation.3 | async-start | bytes 26112000 | tf_op jit(solution)/shard_map/all_gather | solution.py:63
  355.2 5.0 %copy-start.3 = (f32[3200]{0:T(1024)S(1)}, f32[3200]{0:T(1024)}, u32[]{:S(2)}) copy-start(f32[3200]{0:T(1024)} %param.8) | copy-start | bytes 38404
  365.6 3.3 copy-start.2
  393.7 3.6 copy-start.1
Sparse Core Ops, SparseCore 0:
  129.0 70.7 reduce-scatter.1
  202.0 151.1 all-gather.1
